TPU v7x, 512 devices: a whole 4x8x8 slice. The times are simulated.
512 devices in a mesh: dp: 32 (over y, z_hi), seq: 16 (over x, z_lo, core).
Axes of the slice: x: 4, y: 8, z: 8 (z_hi: 4, z_lo: 2; z = z_hi * 2 + z_lo), core: 2. Of those that a mesh axis runs over, the one named last changes fastest.
Arguments:
- queries: bfloat16 [32, 2048, 1024], P('dp', 'seq'), may hold values from -6 to 6
- key_input: bfloat16 [32, 2048, 1024], P('dp', 'seq'), may hold values from -6 to 6
- values: bfloat16 [32, 2048, 1024], P('dp', 'seq'), may hold values from -6 to 6
- cotangent: bfloat16 [32, 2048, 1024], P('dp', 'seq'), may hold values from -12 to 12
- tile_mask: int32 [32, 32, 32], P('dp'), may hold values from 0 to 1, as said below
- condition_flags: int32 [32, 2048], P('dp', 'seq'), may hold values 0 or 1
- condition_embed: float32 [2, 1024], replicated, may hold values from -4 to 4
Outputs:
- attended: bfloat16 [32, 2048, 1024], P('dp', 'seq')
- grad_queries: bfloat16 [32, 2048, 1024], P('dp', 'seq')
- grad_keys: bfloat16 [32, 2048, 1024], P('dp', 'seq')
- grad_values: bfloat16 [32, 2048, 1024], P('dp', 'seq')
- grad_condition: float32 [2, 1024], replicated
Inputs may be any that keep to these rules, and one draw needn't show every extreme that they name: tile_mask[b, i, i] is 1; tile_mask[b, i, j] is 0 unless j < 2 or the absolute difference of i // 2 and j // 2 is at most 1.
All inputs are finite; a program needn't handle non-finite values. No bound on the sum of `condition_flags` on one device may be relied on, other than what follows from the above.
Results may differ from a plain program's by a relative error of at most 0.008.
The roundings to bfloat16 on the way count: a program that leaves them out, or rounds other values in their place, can miss the bound.
Values may be sent and summed in bfloat16 or wider, within the bound.
No kernel may reach another device: no remote copies, remote signals or barrier semaphores. Data moves between devices by JAX's collectives and lax.ppermute only.
A program may use at most 64 MiB of HBM per device.

v0:
```python
import math
import jax
import jax.numpy as jnp
from jax import lax
from jax.sharding import PartitionSpec as P

HEAD_DIM = 128
BLOCK = 64
masked_score = -1e30


def contract_last(left, right):
    return lax.dot_general(
        left, right, (((1,), (1,)), ((), ())), preferred_element_type=jnp.float32
    )


def contract_first(left, right):
    return lax.dot_general(
        left, right, (((0,), (0,)), ((), ())), preferred_element_type=jnp.float32
    )


def attend_and_grads(query_eff, grad_rows, key_set, value_set, allowed, head_count, head_dim):
    score_scale = 1.0 / math.sqrt(head_dim)
    outputs = []
    log_list = []
    delta_list = []
    query_grads = []
    key_grads = []
    value_grads = []
    for head in range(head_count):
        first_col = head * head_dim
        last_col = first_col + head_dim
        scores = jnp.where(
            allowed,
            contract_last(query_eff[:, first_col:last_col], key_set[:, first_col:last_col])
            * score_scale,
            masked_score,
        )
        top = jnp.max(scores, axis=1, keepdims=True)
        total = jnp.sum(jnp.where(allowed, jnp.exp(scores - top), 0.0), axis=1, keepdims=True)
        log_total = top + jnp.log(total)
        weights = jnp.where(allowed, jnp.exp(scores - log_total), 0.0)
        weights_half = weights.astype(jnp.bfloat16)
        output = jnp.dot(
            weights_half, value_set[:, first_col:last_col], preferred_element_type=jnp.float32
        ).astype(jnp.bfloat16)
        head_grad = grad_rows[:, first_col:last_col]
        delta = jnp.sum(
            head_grad.astype(jnp.float32) * output.astype(jnp.float32), axis=1, keepdims=True
        )
        dprob = contract_last(head_grad, value_set[:, first_col:last_col])
        dscore = (weights * (dprob - delta) * score_scale).astype(jnp.bfloat16)
        query_grads.append(
            jnp.dot(dscore, key_set[:, first_col:last_col], preferred_element_type=jnp.float32)
        )
        key_grads.append(contract_first(dscore, query_eff[:, first_col:last_col]))
        value_grads.append(contract_first(weights_half, head_grad))
        outputs.append(output)
        log_list.append(log_total)
        delta_list.append(delta)
    return (
        jnp.concatenate(outputs, axis=1),
        jnp.concatenate(log_list, axis=1),
        jnp.concatenate(delta_list, axis=1),
        jnp.concatenate(query_grads, axis=1),
        jnp.concatenate(key_grads, axis=1),
        jnp.concatenate(value_grads, axis=1),
    )


def head_grads(
    query_eff, grad_rows, key_set, value_set, allowed, log_totals, deltas, head_count, head_dim
):
    score_scale = 1.0 / math.sqrt(head_dim)
    key_grads = []
    value_grads = []
    for head in range(head_count):
        first_col = head * head_dim
        last_col = first_col + head_dim
        scores = jnp.where(
            allowed,
            contract_last(query_eff[:, first_col:last_col], key_set[:, first_col:last_col])
            * score_scale,
            masked_score,
        )
        weights = jnp.where(allowed, jnp.exp(scores - log_totals[:, head : head + 1]), 0.0)
        dprob = contract_last(grad_rows[:, first_col:last_col], value_set[:, first_col:last_col])
        dscore = (weights * (dprob - deltas[:, head : head + 1]) * score_scale).astype(jnp.bfloat16)
        key_grads.append(contract_first(dscore, query_eff[:, first_col:last_col]))
        value_grads.append(
            contract_first(weights.astype(jnp.bfloat16), grad_rows[:, first_col:last_col])
        )
    return (jnp.concatenate(key_grads, axis=1), jnp.concatenate(value_grads, axis=1))


def expand_tiles(tiles, block_rows):
    return jnp.repeat(jnp.repeat(tiles, block_rows, axis=0), block_rows, axis=1) > 0


def body(queries, key_input, values, cotangent, tile_mask, condition_flags, condition_embed):
    graph_count = queries.shape[0] * lax.axis_size("dp")
    query_rows = queries[0]
    key_rows = key_input[0]
    value_rows = values[0]
    grad_rows = cotangent[0]
    tok_rows, width = query_rows.shape
    head_dim = HEAD_DIM
    head_count = width // head_dim
    block_rows = BLOCK
    query_blocks = tok_rows // block_rows
    seq_index = lax.axis_index("seq")
    seq_count = lax.axis_size("seq")
    flag_column = condition_flags[0].astype(jnp.float32)[:, None]
    query_eff = (query_rows.astype(jnp.float32) + flag_column * condition_embed[0][None, :]).astype(
        jnp.bfloat16
    )
    key_eff = (key_rows.astype(jnp.float32) + flag_column * condition_embed[1][None, :]).astype(
        jnp.bfloat16
    )
    tile_table = tile_mask[0]
    block_count = tile_table.shape[0]
    own_tiles = lax.dynamic_slice_in_dim(tile_table, seq_index * query_blocks, query_blocks, 0)
    slot_starts = [
        0,
        (seq_index - 1) * query_blocks,
        seq_index * query_blocks,
        (seq_index + 1) * query_blocks,
    ]
    slot_valid = [seq_index >= 2, seq_index >= 1, seq_index >= 0, seq_index <= seq_count - 2]
    slot_blocks = []
    slot_tiles = []
    for slot in range(4):
        start_block = jnp.clip(slot_starts[slot], 0, block_count - query_blocks)
        slot_blocks.append(start_block)
        columns = lax.dynamic_slice_in_dim(own_tiles, start_block, query_blocks, 1)
        slot_tiles.append(jnp.where(slot_valid[slot], columns, 0))
    allowed = expand_tiles(jnp.concatenate(slot_tiles, axis=1), block_rows)
    whole_keys, whole_values = (
        lax.all_gather(key_eff, "seq", axis=0, tiled=True),
        lax.all_gather(value_rows, "seq", axis=0, tiled=True),
    )
    key_set = jnp.concatenate(
        [
            lax.dynamic_slice_in_dim(whole_keys, slot_blocks[slot] * block_rows, tok_rows, 0)
            for slot in range(4)
        ],
        axis=0,
    )
    value_set = jnp.concatenate(
        [
            lax.dynamic_slice_in_dim(whole_values, slot_blocks[slot] * block_rows, tok_rows, 0)
            for slot in range(4)
        ],
        axis=0,
    )
    attended, log_totals, deltas, query_total, unused_keys, unused_values = attend_and_grads(
        query_eff, grad_rows, key_set, value_set, allowed, head_count, head_dim
    )
    partial_value = jnp.sum(flag_column * query_total, axis=0)
    all_logs, all_deltas = (
        lax.all_gather(log_totals, "seq", axis=0, tiled=True),
        lax.all_gather(deltas, "seq", axis=0, tiled=True),
    )
    own_columns = lax.dynamic_slice_in_dim(tile_table, seq_index * query_blocks, query_blocks, 1)
    allowed_columns = expand_tiles(own_columns, block_rows)
    query_piece = lax.all_gather(query_eff, "seq", axis=0, tiled=True)
    grad_piece = lax.all_gather(grad_rows, "seq", axis=0, tiled=True)
    grads = head_grads(
        query_piece,
        grad_piece,
        key_eff,
        value_rows,
        allowed_columns,
        all_logs,
        all_deltas,
        head_count,
        head_dim,
    )
    key_total = grads[0]
    value_total = grads[1]
    key_partial = jnp.sum(flag_column * key_total, axis=0)
    cond_grad = lax.psum(jnp.stack([partial_value, key_partial]), ("dp", "seq"))
    cond_grad = cond_grad / graph_count
    return (
        attended[None],
        query_total.astype(jnp.bfloat16)[None],
        key_total.astype(jnp.bfloat16)[None],
        value_total.astype(jnp.bfloat16)[None],
        cond_grad,
    )


def solution(mesh):
    placed = (
        P("dp", "seq", None),
        P("dp", "seq", None),
        P("dp", "seq", None),
        P("dp", "seq", None),
        P("dp", None, None),
        P("dp", "seq"),
        P(),
    )
    return jax.shard_map(
        body,
        mesh=mesh,
        in_specs=placed,
        out_specs=(
            P("dp", "seq", None),
            P("dp", "seq", None),
            P("dp", "seq", None),
            P("dp", "seq", None),
            P(),
        ),
        check_vma=False,
    )
```

profile of v0, /device:TPU:1, one launch (start us, length us, event | category | flops | bytes accessed | tf_op | source)
XLA Modules:
  0.0 366.1 jit_solution(12846601326392642082)
XLA Ops:
  14.2 1.8 copy.154
  19.6 50.2 %all-gather.7.cloned.1.call-done = bf16[2048,1024]{0,1:T(8,128)(2,1)} async-done(((bf16[128,1024]{0,1:T(8,128)(2,1)}), bf16[2048,1024]{0,1:T(8,128)(2,1)}) %all-gather.7.cloned.1.call-update) | async-done | bytes 4194320 | tf_op jit(solution)/shard_map/all_gather | solution.py:141
  69.8 1.9 fusion.386
  72.4 41.4 %all-gather.11.cloned.1.call-done = bf16[1,2048,1024]{2,1,0:T(8,128)(2,1)} async-done(((bf16[1,128,1024]{2,1,0:T(8,128)(2,1)}), bf16[1,2048,1024]{2,1,0:T(8,128)(2,1)}) %all-gather.11.cloned.1.call-update) | async-done | bytes 4194320 | tf_op jit(solution)/shard_map/all_gather | solution.py:142
  128.1 1.8 copy.180
  129.9 1.7 multiply_reduce_fusion.2
  131.6 2.0 constant_dynamic-update-slice_fusion.15
  133.6 2.0 constant_dynamic-update-slice_fusion.14
  135.5 2.0 constant_dynamic-update-slice_fusion.13
  137.6 1.8 constant_dynamic-update-slice_fusion.12
  139.4 1.8 constant_dynamic-update-slice_fusion.11
  141.2 1.8 constant_dynamic-update-slice_fusion.10
  143.0 1.9 constant_dynamic-update-slice_fusion.9
  144.9 1.8 constant_dynamic-update-slice_fusion.8
  146.7 1.8 copy.181
  149.9 18.5 %all_gather.21 = f32[2048,8]{0,1:T(8,128)S(1)} all-gather(f32[128,8]{0,1:T(8,128)S(1)} %concatenate.116), channel_id=1, replica_groups=mesh['dp'=32,'seq'=16] {'seq'}, dimensions={0}, use_global_device_ids=true | all-gather | bytes 69632 | tf_op jit(solution)/shard_map/all_gather | solution.py:163
  168.4 16.7 %all_gather.23 = f32[2048,8]{0,1:T(8,128)S(1)} all-gather(f32[128,8]{0,1:T(8,128)S(1)} %concatenate.117), channel_id=1, replica_groups=mesh['dp'=32,'seq'=16] {'seq'}, dimensions={0}, use_global_device_ids=true | all-gather | bytes 69632 | tf_op jit(solution)/shard_map/all_gather | solution.py:164
  189.5 22.6 %all-gather.13.cloned.1.call-done = bf16[1,2048,1024]{2,1,0:T(8,128)(2,1)} async-done(((bf16[1,128,1024]{2,1,0:T(8,128)(2,1)}), bf16[1,2048,1024]{2,1,0:T(8,128)(2,1)}) %all-gather.13.cloned.1.call-update) | async-done | bytes 4194320 | tf_op jit(solution)/shard_map/all_gather | solution.py:169
  215.1 1.8 fusion.115
  218.5 1.8 fusion.117
  222.0 1.8 fusion.119
  225.4 1.8 fusion.121
  228.9 1.8 fusion.123
  237.6 2.4 constant_dynamic-update-slice_fusion.23
  240.1 2.9 constant_dynamic-update-slice_fusion.22
  242.9 2.8 constant_dynamic-update-slice_fusion.21
  245.7 2.8 constant_dynamic-update-slice_fusion.20
  248.5 2.8 constant_dynamic-update-slice_fusion.19
  251.3 2.5 constant_dynamic-update-slice_fusion.18
  253.9 2.5 constant_dynamic-update-slice_fusion.17
  256.4 1.9 constant_dynamic-update-slice_fusion.16
  260.7 98.3 %psum.7 = f32[2,1024]{1,0:T(2,128)S(1)} all-reduce(f32[2,1024]{1,0:T(2,128)S(1)} %pad_maximum_fusion.2), channel_id=1, replica_groups=mesh['dp'=32,'seq'=16] {'dp','seq'}, use_global_device_ids=true, to_apply=%region_26.27 | all-reduce | flops 2048 | bytes 16384 | tf_op jit(solution)/shard_map/psum | solution.py:184
  (153 shorter events, 50.6 us)
Async XLA Ops:
  7.2 62.6 %all-gather.7.cloned.1.call-start = ((), (), s32[]{:S(2)}) async-start(), calls=%async_computation | async-start | bytes 4456448 | tf_op jit(solution)/shard_map/all_gather | solution.py:141
  7.9 63.8 %copy-start.31 = (f32[128]{0:T(128)}, f32[128]{0:T(128)S(1)}, u32[]{:S(2)}) copy-start(f32[128]{0:T(128)S(1)} %convert_bitcast_fusion) | copy-start | bytes 1540
  12.0 59.7 %copy-start.3 = (bf16[128,1024]{0,1:T(8,128)(2,1)S(1)}, bf16[128,1024]{0,1:T(8,128)(2,1)}, u32[]{:S(2)}) copy-start(bf16[128,1024]{0,1:T(8,128)(2,1)} %get-tuple-element.73) | copy-start | bytes 786436
  12.1 101.7 %all-gather.11.cloned.1.call-start = ((), (), s32[]{:S(2)}) async-start(), calls=%async_computation.2 | async-start | bytes 4456448 | tf_op jit(solution)/shard_map/all_gather | solution.py:142
  12.8 174.4 %all-gather.9.cloned.1.call-start = ((), (), s32[]{:S(2)}) async-start(), calls=%async_computation.1 | async-start | bytes 4456448 | tf_op jit(solution)/shard_map/all_gather | solution.py:168
  13.6 198.5 %all-gather.13.cloned.1.call-start = ((), (), s32[]{:S(2)}) async-start(), calls=%async_computation.3 | async-start | bytes 4456448 | tf_op jit(solution)/shard_map/all_gather | solution.py:169
  117.8 4.8 %copy-start = (f32[128,512]{1,0:T(8,128)}, f32[128,512]{1,0:T(8,128)S(1)}, u32[]{:S(2)}) copy-start(f32[128,512]{1,0:T(8,128)S(1)} %get-tuple-element.88) | copy-start | bytes 786436
  118.9 4.6 %copy-start.1 = (f32[128,512]{1,0:T(8,128)}, f32[128,512]{1,0:T(8,128)S(1)}, u32[]{:S(2)}) copy-start(f32[128,512]{1,0:T(8,128)S(1)} %get-tuple-element.90) | copy-start | bytes 786436
  120.0 3.5 copy-start.2
  120.7 2.8 copy-start.27
  120.7 3.7 %copy-start.28 = (f32[128]{0:T(128)}, f32[128]{0:T(128)S(1)}, u32[]{:S(2)}) copy-start(f32[128]{0:T(128)S(1)} %get-tuple-element.144) | copy-start | bytes 1540
  120.8 3.7 copy-start.29
  139.4 47.8 %copy-start.11 = (pred[2048,128]{1,0:T(32,128)(4,1)S(1)}, pred[2048,128]{1,0:T(32,128)(4,1)}, u32[]{:S(2)}) copy-start(pred[2048,128]{1,0:T(32,128)(4,1)} %copy.165) | copy-start | bytes 786436
  143.0 70.4 %copy-start.12 = (pred[2048,128]{1,0:T(32,128)(4,1)S(1)}, pred[2048,128]{1,0:T(32,128)(4,1)}, u32[]{:S(2)}) copy-start(pred[2048,128]{1,0:T(32,128)(4,1)} %copy.165) | copy-start | bytes 786436
  223.7 6.9 %copy-start.13 = (pred[2048,128]{1,0:T(32,128)(4,1)S(1)}, pred[2048,128]{1,0:T(32,128)(4,1)}, u32[]{:S(2)}) copy-start(pred[2048,128]{1,0:T(32,128)(4,1)} %copy.165) | copy-start | bytes 786436
  227.2 6.5 %copy-start.26 = (f32[2048,1]{0,1:T(1,128)S(1)}, f32[2048,1]{0,1:T(1,128)}, u32[]{:S(2)}) copy-start(f32[2048,1]{0,1:T(1,128)} %get-tuple-element.59) | copy-start | bytes 24580
  228.9 4.8 %copy-start.4 = (f32[2048,128]{1,0:T(8,128)}, f32[2048,128]{1,0:T(8,128)S(1)}, u32[]{:S(2)}) copy-start(f32[2048,128]{1,0:T(8,128)S(1)} %fusion.17) | copy-start | bytes 3145732
  240.1 11.3 %copy-start.5 = (f32[2048,128]{1,0:T(8,128)S(1)}, f32[2048,128]{1,0:T(8,128)}, u32[]{:S(2)}) copy-start(f32[2048,128]{1,0:T(8,128)} %copy-done.4) | copy-start | bytes 3145732
  251.3 8.6 %copy-start.14 = (f32[128,128]{0,1:T(8,128)S(1)}, f32[128,128]{0,1:T(8,128)}, u32[]{:S(2)}) copy-start(f32[128,128]{0,1:T(8,128)} %get-tuple-element.112) | copy-start | bytes 196612
  253.8 6.1 %copy-start.10 = (f32[128,1024]{0,1:T(8,128)S(1)}, f32[128,1024]{0,1:T(8,128)}, u32[]{:S(2)}) copy-start(f32[128,1024]{0,1:T(8,128)} %constant_dynamic-update-slice_fusion.31) | copy-start | bytes 1572868
  253.8 6.2 %copy-start.15 = (f32[128,128]{0,1:T(8,128)S(1)}, f32[128,128]{0,1:T(8,128)}, u32[]{:S(2)}) copy-start(f32[128,128]{0,1:T(8,128)} %get-tuple-element.114) | copy-start | bytes 196612
  253.8 6.2 %copy-start.16 = (f32[128,128]{0,1:T(8,128)S(1)}, f32[128,128]{0,1:T(8,128)}, u32[]{:S(2)}) copy-start(f32[128,128]{0,1:T(8,128)} %get-tuple-element.116) | copy-start | bytes 196612
  253.8 6.2 %copy-start.17 = (f32[128,128]{0,1:T(8,128)S(1)}, f32[128,128]{0,1:T(8,128)}, u32[]{:S(2)}) copy-start(f32[128,128]{0,1:T(8,128)} %get-tuple-element.118) | copy-start | bytes 196612
  253.8 6.2 %copy-start.18 = (f32[128,128]{0,1:T(8,128)S(1)}, f32[128,128]{0,1:T(8,128)}, u32[]{:S(2)}) copy-start(f32[128,128]{0,1:T(8,128)} %get-tuple-element.120) | copy-start | bytes 196612
  253.8 6.3 %copy-start.19 = (f32[128,128]{0,1:T(8,128)S(1)}, f32[128,128]{0,1:T(8,128)}, u32[]{:S(2)}) copy-start(f32[128,128]{0,1:T(8,128)} %get-tuple-element.122) | copy-start | bytes 196612
  253.8 6.3 %copy-start.20 = (f32[128,128]{0,1:T(8,128)S(1)}, f32[128,128]{0,1:T(8,128)}, u32[]{:S(2)}) copy-start(f32[128,128]{0,1:T(8,128)} %get-tuple-element.126) | copy-start | bytes 196612
  253.9 6.3 %copy-start.21 = (f32[128,128]{0,1:T(8,128)S(1)}, f32[128,128]{0,1:T(8,128)}, u32[]{:S(2)}) copy-start(f32[128,128]{0,1:T(8,128)} %get-tuple-element.128) | copy-start | bytes 196612
  253.9 6.3 %copy-start.22 = (f32[128,128]{0,1:T(8,128)S(1)}, f32[128,128]{0,1:T(8,128)}, u32[]{:S(2)}) copy-start(f32[128,128]{0,1:T(8,128)} %get-tuple-element.130) | copy-start | bytes 196612
  256.4 3.8 %copy-start.23 = (f32[128,128]{0,1:T(8,128)S(1)}, f32[128,128]{0,1:T(8,128)}, u32[]{:S(2)}) copy-start(f32[128,128]{0,1:T(8,128)} %get-tuple-element.132) | copy-start | bytes 196612
  256.4 3.8 %copy-start.24 = (f32[128,128]{0,1:T(8,128)S(1)}, f32[128,128]{0,1:T(8,128)}, u32[]{:S(2)}) copy-start(f32[128,128]{0,1:T(8,128)} %get-tuple-element.134) | copy-start | bytes 196612
  256.4 3.9 %copy-start.25 = (f32[128,128]{0,1:T(8,128)S(1)}, f32[128,128]{0,1:T(8,128)}, u32[]{:S(2)}) copy-start(f32[128,128]{0,1:T(8,128)} %get-tuple-element.136) | copy-start | bytes 196612
  256.4 3.9 %copy-start.32 = (f32[128]{0:T(128)S(1)}, f32[128]{0:T(128)}, u32[]{:S(2)}) copy-start(f32[128]{0:T(128)} %copy-done.31) | copy-start | bytes 1540
  (5 other events, 8.1 us)
Sparse Core Ops, SparseCore 0:
  12.2 57.5 all-gather.6
  71.9 41.7 all-gather.10
  116.4 51.6 all-gather.8
  170.1 41.9 all-gather.12
where the time goes:
time: 368 us; the launch traced here: 366 us
  blocking collectives  133 us (36%)
  waiting for transfers between devices  116 us (32%)
  matrix products  74.5 us (20%)
  local copies, waits for them, and re-layouts  20.3 us (6%)
  between operations  14.5 us (4%)
  other arithmetic  7.21 us (2%)
    psum x1, blocking collectives, body(): cond_grad = lax.psum(jnp.stack([partial_value, key_partial]), ('dp', 'seq'))  98.3 us
    all_gather x1, waiting for transfers between devices, body(): lax.all_gather(key_eff, 'seq', axis=0, tiled=True)  50.2 us
    all_gather x1, waiting for transfers between devices, body(): lax.all_gather(value_rows, 'seq', axis=0, tiled=True)  41.4 us
    dot_general x16, matrix products, contract_first(): lax.dot_general(left, right, (((0,), (0,)), ((), ())), preferred_element_...  33.7 us
    all_gather x1, waiting for transfers between devices, body(): grad_piece = lax.all_gather(grad_rows, 'seq', axis=0, tiled=True)  22.6 us
    all_gather x1, blocking collectives, body(): lax.all_gather(log_totals, 'seq', axis=0, tiled=True)  18.5 us
    dot_general x16, matrix products, contract_last(): lax.dot_general(left, right, (((1,), (1,)), ((), ())), preferred_element_...  18.5 us
    all_gather x1, blocking collectives, body(): lax.all_gather(deltas, 'seq', axis=0, tiled=True)  16.7 us
  transfers between devices with their start and end apart: 4, of which 3 were waited for; matrix products, arithmetic and copies ran while one was open for 13% of the time, Pallas kernels for 0%

commit v1 on v0

--- a/solution.py
+++ b/solution.py
@@ -181,7 +181,9 @@
     key_total = grads[0]
     value_total = grads[1]
     key_partial = jnp.sum(flag_column * key_total, axis=0)
-    cond_grad = lax.psum(jnp.stack([partial_value, key_partial]), ("dp", "seq"))
+    cond_grad = jnp.sum(
+        lax.all_gather(jnp.stack([partial_value, key_partial]), ("dp", "seq")), axis=0
+    )
     cond_grad = cond_grad / graph_count
     return (
         attended[None],

time: 368 us -> 1090 us (2.96)
  waiting for transfers between devices: 116 us -> 932 us
  blocking collectives: 133 us -> 36.8 us
    all_gather x0 -> x1, waiting for transfers between devices: none -> 806 us  [body(): lax.all_gather(jnp.stack([partial_value, key_partial]), ('dp', 'seq'))]
    psum x1 -> x0, blocking collectives: 98.3 us -> none  [body(): cond_grad = lax.psum(jnp.stack([partial_value, key_partial]), ('dp', 'seq'))]
    all_gather x1, waiting for transfers between devices: 22.6 us -> 35.4 us  [body(): grad_piece = lax.all_gather(grad_rows, 'seq', axis=0, tiled=True)]
  transfers between devices with their start and end apart: 4 -> 5, of which waited for: 3 -> 4; matrix products, arithmetic and copies ran while one was open for 13% -> 4% of each run, Pallas kernels for 0% -> 0%
where the time goes in v1:
time: 1090 us
  waiting for transfers between devices  932 us (86%)
  matrix products  67.9 us (6%)
  blocking collectives  36.8 us (3%)
  local copies, waits for them, and re-layouts  25.4 us (2%)
  between operations  14.5 us (1%)
    all_gather x1, waiting for transfers between devices, body(): lax.all_gather(jnp.stack([partial_value, key_partial]), ('dp', 'seq'))  806 us
    all_gather x1, waiting for transfers between devices, body(): lax.all_gather(key_eff, 'seq', axis=0, tiled=True)  50.1 us
    all_gather x1, waiting for transfers between devices, body(): lax.all_gather(value_rows, 'seq', axis=0, tiled=True)  38.7 us
    all_gather x1, waiting for transfers between devices, body(): grad_piece = lax.all_gather(grad_rows, 'seq', axis=0, tiled=True)  35.4 us
    dot_general x16, matrix products, contract_first(): lax.dot_general(left, right, (((0,), (0,)), ((), ())), preferred_element_...  29.2 us
  transfers between devices with their start and end apart: 5, of which 4 were waited for; matrix products, arithmetic and copies ran while one was open for 4% of the time, Pallas kernels for 0%

profile of v1, /device:TPU:1, one launch (start us, length us, event | category | flops | bytes accessed | tf_op | source)
XLA Modules:
  0.0 1087.4 jit_solution(18270756025777154360)
XLA Ops:
  14.2 1.8 copy.211
  19.7 50.1 %all-gather.10.cloned.1.call-done = bf16[2048,1024]{0,1:T(8,128)(2,1)} async-done(((bf16[128,1024]{0,1:T(8,128)(2,1)}), bf16[2048,1024]{0,1:T(8,128)(2,1)}) %all-gather.10.cloned.1.call-update) | async-done | bytes 4194320 | tf_op jit(solution)/shard_map/all_gather | solution.py:141
  69.8 1.8 fusion.386
  75.1 38.7 %all-gather.14.cloned.1.call-done = bf16[1,2048,1024]{2,1,0:T(8,128)(2,1)} async-done(((bf16[1,128,1024]{2,1,0:T(8,128)(2,1)}), bf16[1,2048,1024]{2,1,0:T(8,128)(2,1)}) %all-gather.14.cloned.1.call-update) | async-done | bytes 4194320 | tf_op jit(solution)/shard_map/all_gather | solution.py:142
  119.0 20.0 %all_gather.27 = f32[2048,8]{0,1:T(8,128)} all-gather(f32[128,8]{0,1:T(8,128)S(1)} %concatenate.116), channel_id=1, replica_groups=mesh['dp'=32,'seq'=16] {'seq'}, dimensions={0}, use_global_device_ids=true | all-gather | bytes 69632 | tf_op jit(solution)/shard_map/all_gather | solution.py:163
  139.0 16.8 %all_gather.29 = f32[2048,8]{0,1:T(8,128)S(1)} all-gather(f32[128,8]{0,1:T(8,128)S(1)} %concatenate.117), channel_id=1, replica_groups=mesh['dp'=32,'seq'=16] {'seq'}, dimensions={0}, use_global_device_ids=true | all-gather | bytes 69632 | tf_op jit(solution)/shard_map/all_gather | solution.py:164
  155.8 2.0 constant_dynamic-update-slice_fusion.15
  159.3 2.0 constant_dynamic-update-slice_fusion.14
  161.3 2.0 constant_dynamic-update-slice_fusion.13
  163.3 1.8 constant_dynamic-update-slice_fusion.12
  165.1 1.8 constant_dynamic-update-slice_fusion.11
  166.9 1.9 constant_dynamic-update-slice_fusion.10
  168.8 1.8 constant_dynamic-update-slice_fusion.9
  170.6 1.8 constant_dynamic-update-slice_fusion.8
  172.4 1.9 fusion.388
  176.7 35.4 %all-gather.16.cloned.1.call-done = bf16[1,2048,1024]{2,1,0:T(8,128)(2,1)} async-done(((bf16[1,128,1024]{2,1,0:T(8,128)(2,1)}), bf16[1,2048,1024]{2,1,0:T(8,128)(2,1)}) %all-gather.16.cloned.1.call-update) | async-done | bytes 4194320 | tf_op jit(solution)/shard_map/all_gather | solution.py:169
  212.1 2.4 constant_dynamic-update-slice_fusion.23
  217.7 2.4 constant_dynamic-update-slice_fusion.22
  222.5 2.4 constant_dynamic-update-slice_fusion.21
  225.6 2.8 fusion.29
  228.4 2.8 constant_dynamic-update-slice_fusion.20
  231.8 2.8 fusion.23
  234.5 2.8 constant_dynamic-update-slice_fusion.19
  237.9 2.7 fusion.17
  240.7 2.8 constant_dynamic-update-slice_fusion.18
  244.1 2.7 fusion.11
  246.8 2.8 constant_dynamic-update-slice_fusion.17
  250.2 2.7 fusion.5
  253.0 2.8 constant_dynamic-update-slice_fusion.16
  262.8 1.9 fusion.115
  271.1 805.8 %all-gather.18.cloned.1.call-done = f32[512,2,1024]{2,1,0:T(2,128)} async-done(((f32[1,2,1024]{2,1,0:T(2,128)}), f32[512,2,1024]{2,1,0:T(2,128)}) %all-gather.18.cloned.1.call-update) | async-done | bytes 4194320 | tf_op jit(solution)/shard_map/all_gather | solution.py:185
  1076.9 3.4 reduce_sum.189
  (192 shorter events, 45.5 us)
Async XLA Ops:
  7.2 62.6 %all-gather.10.cloned.1.call-start = ((), (), s32[]{:S(2)}) async-start(), calls=%async_computation | async-start | bytes 4456448 | tf_op jit(solution)/shard_map/all_gather | solution.py:141
  7.9 63.7 %copy-start.40 = (f32[128]{0:T(128)}, f32[128]{0:T(128)S(1)}, u32[]{:S(2)}) copy-start(f32[128]{0:T(128)S(1)} %convert_bitcast_fusion) | copy-start | bytes 1540
  12.0 59.7 %copy-start.7 = (bf16[128,1024]{0,1:T(8,128)(2,1)S(1)}, bf16[128,1024]{0,1:T(8,128)(2,1)}, u32[]{:S(2)}) copy-start(bf16[128,1024]{0,1:T(8,128)(2,1)} %get-tuple-element.78) | copy-start | bytes 786436
  12.1 101.7 %all-gather.14.cloned.1.call-start = ((), (), s32[]{:S(2)}) async-start(), calls=%async_computation.2 | async-start | bytes 4456448 | tf_op jit(solution)/shard_map/all_gather | solution.py:142
  12.8 161.5 %all-gather.12.cloned.1.call-start = ((), (), s32[]{:S(2)}) async-start(), calls=%async_computation.1 | async-start | bytes 4456448 | tf_op jit(solution)/shard_map/all_gather | solution.py:168
  13.6 198.6 %all-gather.16.cloned.1.call-start = ((), (), s32[]{:S(2)}) async-start(), calls=%async_computation.3 | async-start | bytes 4456448 | tf_op jit(solution)/shard_map/all_gather | solution.py:169
  14.1 1062.7 %all-gather.18.cloned.1.call-start = ((), (), s32[]{:S(2)}) async-start(), calls=%async_computation.4 | async-start | bytes 4202496 | tf_op jit(solution)/shard_map/all_gather | solution.py:185
  75.0 42.7 %copy-start.35 = (f32[128]{0:T(128)}, f32[128]{0:T(128)S(1)}, u32[]{:S(2)}) copy-start(f32[128]{0:T(128)S(1)} %get-tuple-element.147) | copy-start | bytes 1540
  75.0 42.6 %copy-start.36 = (f32[128]{0:T(128)}, f32[128]{0:T(128)S(1)}, u32[]{:S(2)}) copy-start(f32[128]{0:T(128)S(1)} %get-tuple-element.148) | copy-start | bytes 1540
  75.0 42.6 %copy-start.37 = (f32[128]{0:T(128)}, f32[128]{0:T(128)S(1)}, u32[]{:S(2)}) copy-start(f32[128]{0:T(128)S(1)} %get-tuple-element.149) | copy-start | bytes 1540
  75.0 42.6 %copy-start.38 = (f32[128]{0:T(128)}, f32[128]{0:T(128)S(1)}, u32[]{:S(2)}) copy-start(f32[128]{0:T(128)S(1)} %get-tuple-element.150) | copy-start | bytes 1540
  75.1 42.6 %copy-start.39 = (f32[128]{0:T(128)}, f32[128]{0:T(128)S(1)}, u32[]{:S(2)}) copy-start(f32[128]{0:T(128)S(1)} %get-tuple-element.151) | copy-start | bytes 1540
  155.8 14.8 %copy-start.43 = (f32[128]{0:T(128)S(1)}, f32[128]{0:T(128)}, u32[]{:S(2)}) copy-start(f32[128]{0:T(128)} %copy-done.42) | copy-start | bytes 1540
  166.9 48.2 %copy-start.14 = (f32[128,1024]{0,1:T(8,128)S(1)}, f32[128,1024]{0,1:T(8,128)}, u32[]{:S(2)}) copy-start(f32[128,1024]{0,1:T(8,128)} %constant_dynamic-update-slice_fusion.31) | copy-start | bytes 1572868
  168.8 46.4 %copy-start.20 = (f32[128,128]{0,1:T(8,128)S(1)}, f32[128,128]{0,1:T(8,128)}, u32[]{:S(2)}) copy-start(f32[128,128]{0,1:T(8,128)} %get-tuple-element.115) | copy-start | bytes 196612
  168.8 46.4 %copy-start.21 = (f32[128,128]{0,1:T(8,128)S(1)}, f32[128,128]{0,1:T(8,128)}, u32[]{:S(2)}) copy-start(f32[128,128]{0,1:T(8,128)} %get-tuple-element.117) | copy-start | bytes 196612
  168.8 46.4 %copy-start.22 = (f32[128,128]{0,1:T(8,128)S(1)}, f32[128,128]{0,1:T(8,128)}, u32[]{:S(2)}) copy-start(f32[128,128]{0,1:T(8,128)} %get-tuple-element.119) | copy-start | bytes 196612
  168.8 46.4 %copy-start.23 = (f32[128,128]{0,1:T(8,128)S(1)}, f32[128,128]{0,1:T(8,128)}, u32[]{:S(2)}) copy-start(f32[128,128]{0,1:T(8,128)} %get-tuple-element.121) | copy-start | bytes 196612
  170.6 44.6 %copy-start.24 = (f32[128,128]{0,1:T(8,128)S(1)}, f32[128,128]{0,1:T(8,128)}, u32[]{:S(2)}) copy-start(f32[128,128]{0,1:T(8,128)} %get-tuple-element.123) | copy-start | bytes 196612
  170.6 44.6 %copy-start.25 = (f32[128,128]{0,1:T(8,128)S(1)}, f32[128,128]{0,1:T(8,128)}, u32[]{:S(2)}) copy-start(f32[128,128]{0,1:T(8,128)} %get-tuple-element.125) | copy-start | bytes 196612
  172.4 43.7 %copy-start.17 = (pred[2048,128]{1,0:T(32,128)(4,1)S(1)}, pred[2048,128]{1,0:T(32,128)(4,1)}, u32[]{:S(2)}) copy-start(pred[2048,128]{1,0:T(32,128)(4,1)} %copy.222) | copy-start | bytes 786436
  176.1 44.7 %copy-start.13 = (bf16[128,1024]{0,1:T(8,128)(2,1)S(1)}, bf16[128,1024]{0,1:T(8,128)(2,1)}, u32[]{:S(2)}) copy-start(bf16[128,1024]{0,1:T(8,128)(2,1)} %get-tuple-element.79) | copy-start | bytes 786436
  214.5 8.0 copy-start.34
  217.7 7.9 copy-start.31
  220.1 8.2 copy-start.33
  222.5 9.3 copy-start.29
  224.9 9.6 copy-start.32
  228.4 9.6 copy-start.27
  231.1 9.5 copy-start.30
  234.5 9.6 copy-start.26
  237.3 9.5 copy-start.28
  246.8 9.6 copy-start.41
  (24 other events, 58.3 us)
Sparse Core Ops, SparseCore 0:
  12.2 57.5 all-gather.9
  71.9 41.8 all-gather.13
  116.4 52.3 all-gather.11
  170.8 41.2 all-gather.15
  258.7 818.1 all-gather.17
